TPU v7x, 128 devices: a whole 4x4x4 slice. The times are simulated.
128 devices in a mesh: ctx: 16 (over x, y_lo, core), tp: 8 (over y_hi, z).
Axes of the slice: x: 4, y: 4 (y_hi: 2, y_lo: 2; y = y_hi * 2 + y_lo), z: 4, core: 2. Of those that a mesh axis runs over, the one named last changes fastest.
Arguments:
- ctx_queries: bfloat16 [16384, 8192], P('ctx', 'tp'), may hold values from -70 to 70
- context_key_rows: bfloat16 [16384, 1024], P('ctx', 'tp'), may hold values from -4 to 4
- context_value_rows: bfloat16 [16384, 1024], P('ctx', 'tp'), may hold values from -6 to 6
- resp_queries: bfloat16 [512, 8192], P('ctx', 'tp'), may hold values from -70 to 70
- resp_keys: bfloat16 [512, 1024], P('ctx', 'tp'), may hold values from -4 to 4
- response_value_rows: bfloat16 [512, 1024], P('ctx', 'tp'), may hold values from -6 to 6
- split_index: int32 [1], replicated, may hold values from 64 to 448
- out_weight: bfloat16 [8192, 8192], P('tp'), may hold values from -0.0625 to 0.0625
Outputs:
- ctx_out: float32 [16384, 8192], P('ctx', 'tp')
- resp_out: float32 [512, 8192], P('ctx', 'tp')
All inputs are finite; a program needn't handle non-finite values.
Results may differ from a plain program's by a relative error of at most 0.005.
Values may be sent and summed in bfloat16 or wider, within the bound.
No kernel may reach another device: no remote copies, remote signals or barrier semaphores. Data moves between devices by JAX's collectives and lax.ppermute only.
A program may use at most 192 MiB of HBM per device.

v0:
```python
import jax
import jax.numpy as jnp
from jax import lax
from jax.experimental import pallas as pl
from jax.experimental.pallas import tpu as pltpu
from jax.sharding import PartitionSpec as P


HEAD_WIDTH = 128
NEGATIVE = -1e30
SCALE = HEAD_WIDTH ** (-0.5)
INTERPRET = False


def _dot_t(a, b):
    return lax.dot_general(a, b, (((1,), (1,)), ((), ())), preferred_element_type=jnp.float32)


def _ctx_kernel(flag_ref, q_ref, ka_ref, va_ref, ko_ref, vo_ref, o_ref):
    tq = q_ref.shape[0]
    tiles = ko_ref.shape[0] // tq
    i = pl.program_id(1)
    rows = lax.broadcasted_iota(jnp.int32, (tq, tq), 0)
    cols = lax.broadcasted_iota(jnp.int32, (tq, tq), 1)
    diag_vis = cols <= rows

    def tile(c, with_anchor):
        q = q_ref[...]
        parts = []
        if with_anchor:
            parts.append((_dot_t(q, ka_ref[...]) * SCALE, va_ref[...]))
        if c > 0:
            parts.append((_dot_t(q, ko_ref[:c * tq, :]) * SCALE, vo_ref[:c * tq, :]))
        s_d = jnp.where(diag_vis, _dot_t(q, ko_ref[c * tq:(c + 1) * tq, :]) * SCALE, NEGATIVE)
        parts.append((s_d, vo_ref[c * tq:(c + 1) * tq, :]))
        m = parts[0][0].max(axis=1, keepdims=True)
        for sc, _ in parts[1:]:
            m = jnp.maximum(m, sc.max(axis=1, keepdims=True))
        total = None
        num = None
        for sc, vals in parts:
            p = jnp.exp(sc - m)
            t = jnp.sum(p, axis=1, keepdims=True)
            n = jnp.dot(p.astype(jnp.bfloat16), vals, preferred_element_type=jnp.float32)
            total = t if total is None else total + t
            num = n if num is None else num + n
        o_ref[...] = num / total

    on = flag_ref[0] > 0
    for c in range(tiles):
        @pl.when(jnp.logical_and(i == c, on))
        def _(c=c):
            tile(c, True)

        @pl.when(jnp.logical_and(i == c, jnp.logical_not(on)))
        def _(c=c):
            tile(c, False)


def ctx_attention(flag, q, ka, va, ko, vo, head0, nheads, into=None, tq=256):
    rows, width = q.shape
    block = ko.shape[0]
    kv_spec = pl.BlockSpec((block, HEAD_WIDTH), lambda h, i, f: (0, 0))
    in_specs = [
        pl.BlockSpec((tq, HEAD_WIDTH), lambda h, i, f: (i, h + head0)),
        kv_spec, kv_spec, kv_spec, kv_spec,
    ]
    operands = [flag, q, ka, va, ko, vo]
    kernel = _ctx_kernel
    aliases = {}
    if into is not None:
        in_specs.append(pl.BlockSpec(memory_space=pl.ANY))
        operands.append(into)
        aliases = {6: 0}

        def kernel(flag_ref, q_ref, ka_ref, va_ref, ko_ref, vo_ref, into_ref, o_ref):
            _ctx_kernel(flag_ref, q_ref, ka_ref, va_ref, ko_ref, vo_ref, o_ref)

    grid_spec = pltpu.PrefetchScalarGridSpec(
        num_scalar_prefetch=1,
        grid=(nheads, rows // tq),
        in_specs=in_specs,
        out_specs=pl.BlockSpec((tq, HEAD_WIDTH), lambda h, i, f: (i, h + head0)),
    )
    return pl.pallas_call(
        kernel,
        grid_spec=grid_spec,
        out_shape=jax.ShapeDtypeStruct((rows, width), jnp.float32),
        input_output_aliases=aliases,
        interpret=INTERPRET,
    )(*operands)


def _finish_kernel(st_ref, own_ref, w_ref, o_ref, att_ref):
    width = att_ref.shape[1]
    heads = width // HEAD_WIDTH

    @pl.when(pl.program_id(0) == 0)
    def _():
        for h in range(heads):
            hc = slice(h * HEAD_WIDTH, (h + 1) * HEAD_WIDTH)
            mc = slice(width + h, width + h + 1)
            lc = slice(width + heads + h, width + heads + h + 1)
            m_s = st_ref[:, :, mc]
            m_r = own_ref[:, mc]
            top = jnp.maximum(jnp.max(m_s, axis=0), m_r)
            f_s = jnp.exp(m_s - top[None])
            f_r = jnp.exp(m_r - top)
            total = jnp.sum(st_ref[:, :, lc] * f_s, axis=0) + own_ref[:, lc] * f_r
            numer = jnp.sum(st_ref[:, :, hc] * f_s, axis=0) + own_ref[:, hc] * f_r
            att_ref[:, hc] = (numer / total).astype(att_ref.dtype)

    o_ref[...] = jnp.dot(att_ref[...], w_ref[...], preferred_element_type=jnp.float32)


def finish_projection(state, own, w, tn=1024):
    sources, rows, packed = state.shape
    inner, cols = w.shape
    return pl.pallas_call(
        _finish_kernel,
        grid=(cols // tn,),
        in_specs=[
            pl.BlockSpec((sources, rows, packed), lambda j: (0, 0, 0)),
            pl.BlockSpec((rows, packed), lambda j: (0, 0)),
            pl.BlockSpec((inner, tn), lambda j: (0, j)),
        ],
        out_specs=pl.BlockSpec((rows, tn), lambda j: (0, j)),
        out_shape=jax.ShapeDtypeStruct((rows, cols), jnp.float32),
        scratch_shapes=[pltpu.VMEM((rows, inner), jnp.bfloat16)],
        interpret=INTERPRET,
    )(state, own, w)


def _part_kernel(q_ref, k_ref, v_ref, st_ref):
    width = q_ref.shape[1]
    heads = width // HEAD_WIDTH
    k = k_ref[...]
    v = v_ref[...]
    for j in range(heads):
        hc = slice(j * HEAD_WIDTH, (j + 1) * HEAD_WIDTH)
        s = _dot_t(q_ref[:, hc], k) * SCALE
        m = jnp.max(s, axis=1, keepdims=True)
        w = jnp.exp(s - m)
        st_ref[:, width + j:width + j + 1] = m
        st_ref[:, width + heads + j:width + heads + j + 1] = jnp.sum(w, axis=1, keepdims=True)
        st_ref[:, hc] = jnp.dot(w.astype(jnp.bfloat16), v, preferred_element_type=jnp.float32)


def part_attention(q, k, v, tq=128):
    rows = q.shape[0]
    width = q.shape[1]
    heads = width // HEAD_WIDTH
    block = k.shape[0]
    kv_spec = pl.BlockSpec((block, HEAD_WIDTH), lambda i: (0, 0))
    return pl.pallas_call(
        _part_kernel,
        grid=(rows // tq,),
        in_specs=[pl.BlockSpec((tq, width), lambda i: (i, 0)), kv_spec, kv_spec],
        out_specs=pl.BlockSpec((tq, width + 2 * heads), lambda i: (i, 0)),
        out_shape=jax.ShapeDtypeStruct((rows, width + 2 * heads), jnp.float32),
        interpret=INTERPRET,
    )(q, k, v)


def gather_by_all_to_all(x, axis, n):
    copies = jnp.broadcast_to(x[None], (n,) + x.shape)
    return lax.all_to_all(copies, axis, 0, 0).reshape((n * x.shape[0],) + x.shape[1:])


def broadcast_from_first(x, axis, device, n):
    stride = n // 2
    while stride >= 1:
        pairs = [(s, s + stride) for s in range(0, n, 2 * stride)]
        got = lax.ppermute(x, axis, pairs)
        x = jnp.where(device % (2 * stride) == stride, got, x)
        stride //= 2
    return x


def layer(
    ctx_queries,
    context_key_rows,
    context_value_rows,
    resp_queries,
    resp_keys,
    response_value_rows,
    split_index,
    out_weight,
):
    device = lax.axis_index("ctx")
    n_ctx = lax.axis_size("ctx")
    width = resp_queries.shape[1]
    heads = width // HEAD_WIDTH
    resp_dev = resp_queries.shape[0]

    packed = jnp.concatenate([resp_queries, resp_keys, response_value_rows], axis=1)
    gathered = gather_by_all_to_all(packed, "ctx", n_ctx)
    all_q = gathered[:, :width]
    all_k = gathered[:, width:width + HEAD_WIDTH]
    all_v = gathered[:, width + HEAD_WIDTH:]

    state = part_attention(all_q, context_key_rows, context_value_rows)

    anchor = broadcast_from_first(
        jnp.stack([context_key_rows, context_value_rows]), "ctx", device, n_ctx
    )
    anchor, state = lax.optimization_barrier((anchor, state))
    state = lax.all_to_all(state, "ctx", 0, 0, tiled=True)

    flag = (device > 0).astype(jnp.int32).reshape(1)
    kv = (anchor[0], anchor[1], context_key_rows, context_value_rows)
    half = (heads * 5) // 8
    ctx_out = ctx_attention(flag, ctx_queries, *kv, 0, half)
    ctx_out, state = lax.optimization_barrier((ctx_out, state))
    state = state.reshape(n_ctx, resp_dev, -1)

    own_rows = device * resp_dev + jnp.arange(resp_dev, dtype=jnp.int32)
    key_pos = jnp.arange(all_k.shape[0], dtype=jnp.int32)
    boundary = split_index[0]
    seen = (key_pos[None, :] <= own_rows[:, None]) & (
        (key_pos[None, :] < boundary) == (own_rows[:, None] < boundary)
    )
    q_own = resp_queries.reshape(resp_dev, heads, HEAD_WIDTH)
    s_r = jnp.einsum("rhd,kd->rhk", q_own, all_k, preferred_element_type=jnp.float32) * SCALE
    s_r = jnp.where(seen[:, None, :], s_r, NEGATIVE)
    m_r = jnp.max(s_r, axis=2)
    w_r = jnp.where(seen[:, None, :], jnp.exp(s_r - m_r[:, :, None]), 0.0)
    l_r = jnp.sum(w_r, axis=2)
    num_r = jnp.einsum(
        "rhk,kd->rhd", w_r.astype(jnp.bfloat16), all_v, preferred_element_type=jnp.float32
    )
    own = jnp.concatenate([num_r.reshape(resp_dev, width), m_r, l_r], axis=1)
    projected = finish_projection(state, own, out_weight)
    n_tp = lax.axis_size("tp")
    shares = lax.all_to_all(projected, "tp", 1, 0, tiled=True)
    ctx_out = ctx_attention(flag, ctx_queries, *kv, half, heads - half, into=ctx_out)
    ctx_out, shares = lax.optimization_barrier((ctx_out, shares))
    resp_out = jnp.sum(shares.reshape(n_tp, resp_dev, -1), axis=0)
    return (ctx_out, resp_out)


def solution(mesh):
    placed = (
        P("ctx", "tp"),
        P("ctx", "tp"),
        P("ctx", "tp"),
        P("ctx", "tp"),
        P("ctx", "tp"),
        P("ctx", "tp"),
        P(),
        P("tp", None),
    )
    return jax.shard_map(
        layer,
        mesh=mesh,
        in_specs=placed,
        out_specs=(P("ctx", "tp"), P("ctx", "tp")),
        check_vma=False,
    )
```

profile of v0, /device:TPU:8, one launch (start us, length us, event | category | flops | bytes accessed | tf_op | source)
XLA Modules:
  0.0 142.5 jit_solution(8337573229218280618)
XLA Ops:
  0.7 1.1 pad_maximum_fusion
  1.8 0.8 collective-permute-start
  2.7 1.1 broadcast_select_fusion
  4.6 1.3 collective-permute-start.2
  6.0 1.2 broadcast_in_dim.31
  7.2 24.9 %all-to-all-start = ((bf16[16,32,1280]{2,1,0:T(8,128)(2,1)}), bf16[16,32,1280]{2,1,0:T(8,128)(2,1)S(1)}, u32[]{:S(2)}, u32[]{:S(2)}) async-start(bf16[16,32,1280]{2,1,0:T(8,128)(2,1)} %broadcast_in_dim.31), calls=%async_computation | async-start | bytes 2621440 | tf_op jit(solution)/shard_map/all_to_all | solution.py:167
  32.1 2.1 %collective-permute-start.3 = (bf16[2,1024,128]{2,1,0:T(8,128)(2,1)S(1)}, bf16[2,1024,128]{2,1,0:T(8,128)(2,1)S(1)}, u32[]{:S(2)}, u32[]{:S(2)}) collective-permute-start(bf16[2,1024,128]{2,1,0:T(8,128)(2,1)S(1)} %broadcast_select_fusion.2), channel_id=1, source_target_pairs={{0,8},{16,24},{32,40},{48,56},{64,72},{80,88},{96,104},{112,120},{... | collective-permute-start | bytes 1572872 | tf_op jit(solution)/shard_map/ppermute | solution.py:174
  34.2 15.8 %all-to-all-done = bf16[16,32,1280]{2,1,0:T(8,128)(2,1)S(1)} async-done(((bf16[16,32,1280]{2,1,0:T(8,128)(2,1)}), bf16[16,32,1280]{2,1,0:T(8,128)(2,1)S(1)}, u32[]{:S(2)}, u32[]{:S(2)}) %all-to-all-start) | async-done | bytes 1310752 | tf_op jit(solution)/shard_map/all_to_all | solution.py:167
  50.0 1.2 slice.20.q_ref
  51.2 13.9 %shard_map.95 = f32[512,1040]{1,0:T(8,128)} custom-call(bf16[512,1024]{1,0:T(8,128)(2,1)} %slice.20.q_ref, bf16[1024,128]{1,0:T(8,128)(2,1)} %ko_ref.3, bf16[1024,128]{1,0:T(8,128)(2,1)} %vo_ref.3), custom_call_target="tpu_custom_call" | custom-call | tf_op jit(solution)/shard_map/pallas_call | solution.py:155
  65.2 4.9 %all-to-all-start.1 = ((f32[16,32,1040]{2,1,0:T(8,128)}), f32[16,32,1040]{2,1,0:T(8,128)S(1)}, u32[]{:S(2)}, u32[]{:S(2)}) async-start(f32[16,32,1040]{2,1,0:T(8,128)} %bitcast.47), calls=%async_computation.1 | async-start | bytes 4718592 | tf_op jit(solution)/shard_map/all_to_all | solution.py:208
  70.9 1.2 fusion.9
  72.4 1.2 fusion.4
  73.7 0.7 concatenate.7.own_ref
  74.4 0.8 slice_bitcast_fusion
  75.3 23.4 %shard_map.96.into_ref = f32[1024,1024]{1,0:T(8,128)} custom-call(s32[1]{0:T(128)} %bitcast.flag_ref, bf16[1024,1024]{1,0:T(8,128)(2,1)} %q_ref.3, bf16[1024,128]{1,0:T(8,128)(2,1)} %get-tuple-element.17.ka_ref, bf16[1024,128]{1,0:T(8,128)(2,1)} %get-tuple-element.16.va_ref, bf16[1024,128]{1,0:T(8,128)(2,1)} %ko_ref.3, bf16[1024,128]{1,0:T(8,128)(2,1)} %vo_ref.3), custom_call_target="tpu_custom_call" | custom-call | tf_op jit(solution)/shard_map/pallas_call | solution.py:85
  98.7 3.2 %all-to-all-done.1 = f32[16,32,1040]{2,1,0:T(8,128)S(1)} async-done(((f32[16,32,1040]{2,1,0:T(8,128)}), f32[16,32,1040]{2,1,0:T(8,128)S(1)}, u32[]{:S(2)}, u32[]{:S(2)}) %all-to-all-start.1) | async-done | bytes 2129952 | tf_op jit(solution)/shard_map/all_to_all | solution.py:208
  101.9 1.4 copy-done
  103.4 12.3 %shard_map.98 = f32[32,8192]{1,0:T(8,128)} custom-call(f32[16,32,1040]{2,1,0:T(8,128)} %copy-done, f32[32,1040]{1,0:T(8,128)} %concatenate.7.own_ref, bf16[1024,8192]{1,0:T(8,128)(2,1)} %w_ref.1), custom_call_target="tpu_custom_call" | custom-call | tf_op jit(solution)/shard_map/pallas_call | solution.py:119
  115.7 2.3 %copy.36 = f32[4,8,8,1024]{3,2,0,1:T(8,128)} copy(f32[4,8,8,1024]{3,2,1,0:T(8,128)} %bitcast.57) | data formatting | bytes 2097152 | tf_op jit(solution)/shard_map/all_to_all | solution.py:235
  118.0 7.5 %all-to-all-start.2 = ((f32[32,8,1024]{2,0,1:T(8,128)}), f32[32,8,1024]{2,0,1:T(8,128)S(1)}, u32[]{:S(2)}, u32[]{:S(2)}) async-start(f32[32,8,1024]{2,0,1:T(8,128)} %bitcast.43), calls=%async_computation.2 | async-start | bytes 2097152 | tf_op jit(solution)/shard_map/all_to_all | solution.py:235
  125.5 14.9 %shard_map.97 = f32[1024,1024]{1,0:T(8,128)} custom-call(s32[1]{0:T(128)} %bitcast.flag_ref, bf16[1024,1024]{1,0:T(8,128)(2,1)} %q_ref.3, bf16[1024,128]{1,0:T(8,128)(2,1)} %get-tuple-element.17.ka_ref, bf16[1024,128]{1,0:T(8,128)(2,1)} %get-tuple-element.16.va_ref, bf16[1024,128]{1,0:T(8,128)(2,1)} %ko_ref.3, ...), custom_call_target="tpu_custom_call", output_to_operand_aliasing={{}: (6, {})} | custom-call | tf_op jit(solution)/shard_map/pallas_call | solution.py:85
  140.4 1.3 all-to-all-done.2
  141.7 0.7 reduce_sum.19
  (30 shorter events, 1.5 us)
Async XLA Ops:
  0.6 3.9 %copy-start.2 = (bf16[1024,128]{1,0:T(8,128)(2,1)S(1)}, bf16[1024,128]{1,0:T(8,128)(2,1)}, u32[]{:S(2)}) copy-start(bf16[1024,128]{1,0:T(8,128)(2,1)} %ko_ref.3) | copy-start | bytes 786436
  0.6 3.9 %copy-start.1 = (bf16[1024,128]{1,0:T(8,128)(2,1)S(1)}, bf16[1024,128]{1,0:T(8,128)(2,1)}, u32[]{:S(2)}) copy-start(bf16[1024,128]{1,0:T(8,128)(2,1)} %vo_ref.3) | copy-start | bytes 786436
  1.8 4.1 %copy-start.4 = (bf16[32,1024]{1,0:T(8,128)(2,1)S(1)}, bf16[32,1024]{1,0:T(8,128)(2,1)}, u32[]{:S(2)}) copy-start(bf16[32,1024]{1,0:T(8,128)(2,1)} %param.11) | copy-start | bytes 196612
  1.8 4.1 %copy-start.5 = (bf16[32,128]{1,0:T(8,128)(2,1)S(1)}, bf16[32,128]{1,0:T(8,128)(2,1)}, u32[]{:S(2)}) copy-start(bf16[32,128]{1,0:T(8,128)(2,1)} %param.13) | copy-start | bytes 24580
  1.8 4.1 %copy-start.6 = (bf16[32,128]{1,0:T(8,128)(2,1)S(1)}, bf16[32,128]{1,0:T(8,128)(2,1)}, u32[]{:S(2)}) copy-start(bf16[32,128]{1,0:T(8,128)(2,1)} %param.12) | copy-start | bytes 24580
  1.8 0.9 collective-permute-start
  3.8 0.7 collective-permute-start.1
  4.6 27.4 %collective-permute-start.2 = (bf16[2,1024,128]{2,1,0:T(8,128)(2,1)S(1)}, bf16[2,1024,128]{2,1,0:T(8,128)(2,1)S(1)}, u32[]{:S(2)}, u32[]{:S(2)}) collective-permute-start(bf16[2,1024,128]{2,1,0:T(8,128)(2,1)S(1)} %broadcast_select_fusion.1), channel_id=1, source_target_pairs={{0,16},{32,48},{64,80},{96,112},{1,17},{33,49},{65,81},{97,113},{2... | collective-permute-start | bytes 1572872 | tf_op jit(solution)/shard_map/ppermute | solution.py:174
  7.2 42.8 %all-to-all-start = ((bf16[16,32,1280]{2,1,0:T(8,128)(2,1)}), bf16[16,32,1280]{2,1,0:T(8,128)(2,1)S(1)}, u32[]{:S(2)}, u32[]{:S(2)}) async-start(bf16[16,32,1280]{2,1,0:T(8,128)(2,1)} %broadcast_in_dim.31), calls=%async_computation | async-start | bytes 2621440 | tf_op jit(solution)/shard_map/all_to_all | solution.py:167
  32.1 33.0 %collective-permute-start.3 = (bf16[2,1024,128]{2,1,0:T(8,128)(2,1)S(1)}, bf16[2,1024,128]{2,1,0:T(8,128)(2,1)S(1)}, u32[]{:S(2)}, u32[]{:S(2)}) collective-permute-start(bf16[2,1024,128]{2,1,0:T(8,128)(2,1)S(1)} %broadcast_select_fusion.2), channel_id=1, source_target_pairs={{0,8},{16,24},{32,40},{48,56},{64,72},{80,88},{96,104},{112,120},{... | collective-permute-start | bytes 1572872 | tf_op jit(solution)/shard_map/ppermute | solution.py:174
  50.0 15.1 %copy-start.3 = (bf16[16,32,1280]{2,1,0:T(8,128)(2,1)}, bf16[16,32,1280]{2,1,0:T(8,128)(2,1)S(1)}, u32[]{:S(2)}) copy-start(bf16[16,32,1280]{2,1,0:T(8,128)(2,1)S(1)} %all-to-all-done) | copy-start | bytes 3932164
  65.2 36.8 %all-to-all-start.1 = ((f32[16,32,1040]{2,1,0:T(8,128)}), f32[16,32,1040]{2,1,0:T(8,128)S(1)}, u32[]{:S(2)}, u32[]{:S(2)}) async-start(f32[16,32,1040]{2,1,0:T(8,128)} %bitcast.47), calls=%async_computation.1 | async-start | bytes 4718592 | tf_op jit(solution)/shard_map/all_to_all | solution.py:208
  101.9 1.4 copy-start
  118.0 23.7 %all-to-all-start.2 = ((f32[32,8,1024]{2,0,1:T(8,128)}), f32[32,8,1024]{2,0,1:T(8,128)S(1)}, u32[]{:S(2)}, u32[]{:S(2)}) async-start(f32[32,8,1024]{2,0,1:T(8,128)} %bitcast.43), calls=%async_computation.2 | async-start | bytes 2097152 | tf_op jit(solution)/shard_map/all_to_all | solution.py:235
where the time goes:
time: 145 us; the launch traced here: 142 us
  Pallas kernels  64.5 us (44%)
  starting transfers between devices  42.2 us (29%)
  waiting for transfers between devices  20.4 us (14%)
  local copies, waits for them, and re-layouts  7.9 us (5%)
  other arithmetic  3.51 us (2%)
  matrix products  2.39 us (2%)
  between operations  1.55 us (1%)
    pallas_call x2, Pallas kernels, ctx_attention(): pl.pallas_call(kernel, grid_spec=grid_spec, out_shape=jax.ShapeDtypeStruc...  38.3 us
    all_to_all x1, starting transfers between devices, gather_by_all_to_all(): lax.all_to_all(copies, axis, 0, 0).reshape((n * x.shape[0],) + x.shape[1:])  24.9 us
    all_to_all x1, waiting for transfers between devices, gather_by_all_to_all(): lax.all_to_all(copies, axis, 0, 0).reshape((n * x.shape[0],) + x.shape[1:])  15.8 us
    pallas_call x1, Pallas kernels, part_attention(): pl.pallas_call(_part_kernel, grid=(rows // tq,), in_specs=[pl.BlockSpec((...  13.9 us
    pallas_call x1, Pallas kernels, finish_projection(): pl.pallas_call(_finish_kernel, grid=(cols // tn,), in_specs=[pl.BlockSpec...  12.3 us
    all_to_all x1, starting transfers between devices, layer(): shares = lax.all_to_all(projected, 'tp', 1, 0, tiled=True)  7.52 us
    all_to_all x1, starting transfers between devices, layer(): state = lax.all_to_all(state, 'ctx', 0, 0, tiled=True)  4.94 us
    ppermute x4, starting transfers between devices, broadcast_from_first(): got = lax.ppermute(x, axis, pairs)  4.86 us
  transfers between devices with their start and end apart: 7, of which 3 were waited for; matrix products, arithmetic and copies ran while one was open for 5% of the time, Pallas kernels for 37%

commit v1 on v0

--- a/solution.py
+++ b/solution.py
@@ -113,7 +113,7 @@
     o_ref[...] = jnp.dot(att_ref[...], w_ref[...], preferred_element_type=jnp.float32)
 
 
-def finish_projection(state, own, w, tn=1024):
+def finish_projection(state, own, w, tn):
     sources, rows, packed = state.shape
     inner, cols = w.shape
     return pl.pallas_call(
@@ -124,8 +124,8 @@
             pl.BlockSpec((rows, packed), lambda j: (0, 0)),
             pl.BlockSpec((inner, tn), lambda j: (0, j)),
         ],
-        out_specs=pl.BlockSpec((rows, tn), lambda j: (0, j)),
-        out_shape=jax.ShapeDtypeStruct((rows, cols), jnp.float32),
+        out_specs=pl.BlockSpec((None, rows, tn), lambda j: (j, 0, 0)),
+        out_shape=jax.ShapeDtypeStruct((cols // tn, rows, tn), jnp.float32),
         scratch_shapes=[pltpu.VMEM((rows, inner), jnp.bfloat16)],
         interpret=INTERPRET,
     )(state, own, w)
@@ -204,7 +204,6 @@
     anchor = broadcast_from_first(
         jnp.stack([context_key_rows, context_value_rows]), "ctx", device, n_ctx
     )
-    anchor, state = lax.optimization_barrier((anchor, state))
     state = lax.all_to_all(state, "ctx", 0, 0, tiled=True)
 
     flag = (device > 0).astype(jnp.int32).reshape(1)
@@ -230,9 +229,9 @@
         "rhk,kd->rhd", w_r.astype(jnp.bfloat16), all_v, preferred_element_type=jnp.float32
     )
     own = jnp.concatenate([num_r.reshape(resp_dev, width), m_r, l_r], axis=1)
-    projected = finish_projection(state, own, out_weight)
     n_tp = lax.axis_size("tp")
-    shares = lax.all_to_all(projected, "tp", 1, 0, tiled=True)
+    projected = finish_projection(state, own, out_weight, out_weight.shape[1] // n_tp)
+    shares = lax.all_to_all(projected, "tp", 0, 0, tiled=True)
     ctx_out = ctx_attention(flag, ctx_queries, *kv, half, heads - half, into=ctx_out)
     ctx_out, shares = lax.optimization_barrier((ctx_out, shares))
     resp_out = jnp.sum(shares.reshape(n_tp, resp_dev, -1), axis=0)

time: 145 us -> 132 us (0.910)
  the two profiles are of different devices: /device:TPU:8 before, /device:TPU:24 now
where the time goes in v1:
time: 132 us; the launch traced here: 130 us
  Pallas kernels  64.5 us (49%)
  starting transfers between devices  31.6 us (24%)
  waiting for transfers between devices  15.8 us (12%)
  local copies, waits for them, and re-layouts  7.57 us (6%)
  other arithmetic  5.97 us (5%)
  matrix products  3.1 us (2%)
  between operations  1.48 us (1%)
    pallas_call x2, Pallas kernels, ctx_attention(): pl.pallas_call(kernel, grid_spec=grid_spec, out_shape=jax.ShapeDtypeStruc...  38.3 us
    all_to_all x1, waiting for transfers between devices, gather_by_all_to_all(): lax.all_to_all(copies, axis, 0, 0).reshape((n * x.shape[0],) + x.shape[1:])  15.8 us
    pallas_call x1, Pallas kernels, part_attention(): pl.pallas_call(_part_kernel, grid=(rows // tq,), in_specs=[pl.BlockSpec((...  13.9 us
    pallas_call x1, Pallas kernels, finish_projection(): pl.pallas_call(_finish_kernel, grid=(cols // tn,), in_specs=[pl.BlockSpec...  12.3 us
    all_to_all x1, starting transfers between devices, layer(): state = lax.all_to_all(state, 'ctx', 0, 0, tiled=True)  10.6 us
    all_to_all x1, starting transfers between devices, gather_by_all_to_all(): lax.all_to_all(copies, axis, 0, 0).reshape((n * x.shape[0],) + x.shape[1:])  8.51 us
    all_to_all x1, starting transfers between devices, layer(): shares = lax.all_to_all(projected, 'tp', 0, 0, tiled=True)  8.28 us
    ppermute x4, starting transfers between devices, broadcast_from_first(): got = lax.ppermute(x, axis, pairs)  4.13 us
  transfers between devices with their start and end apart: 7, of which 1 were waited for; matrix products, arithmetic and copies ran while one was open for 10% of the time, Pallas kernels for 40%

profile of v1, /device:TPU:24, one launch (start us, length us, event | category | flops | bytes accessed | tf_op | source)
XLA Modules:
  0.0 130.0 jit_solution(12869902576404752159)
XLA Ops:
  0.6 1.1 pad_maximum_fusion
  1.8 0.8 collective-permute-start
  2.6 0.9 pad_maximum_fusion.1
  3.5 1.2 broadcast_in_dim.31
  4.7 8.5 %all-to-all-start = ((bf16[16,32,1280]{2,1,0:T(8,128)(2,1)}), bf16[16,32,1280]{2,1,0:T(8,128)(2,1)S(1)}, u32[]{:S(2)}, u32[]{:S(2)}) async-start(bf16[16,32,1280]{2,1,0:T(8,128)(2,1)} %broadcast_in_dim.31), calls=%async_computation | async-start | bytes 2621440 | tf_op jit(solution)/shard_map/all_to_all | solution.py:167
  14.1 1.3 collective-permute-start.2
  15.4 15.8 %all-to-all-done = bf16[16,32,1280]{2,1,0:T(8,128)(2,1)S(1)} async-done(((bf16[16,32,1280]{2,1,0:T(8,128)(2,1)}), bf16[16,32,1280]{2,1,0:T(8,128)(2,1)S(1)}, u32[]{:S(2)}, u32[]{:S(2)}) %all-to-all-start) | async-done | bytes 1310752 | tf_op jit(solution)/shard_map/all_to_all | solution.py:167
  31.1 1.2 slice.22.q_ref
  32.4 13.9 %shard_map.96 = f32[512,1040]{1,0:T(8,128)} custom-call(bf16[512,1024]{1,0:T(8,128)(2,1)} %slice.22.q_ref, bf16[1024,128]{1,0:T(8,128)(2,1)} %ko_ref.3, bf16[1024,128]{1,0:T(8,128)(2,1)} %vo_ref.3), custom_call_target="tpu_custom_call" | custom-call | tf_op jit(solution)/shard_map/pallas_call | solution.py:155
  46.2 10.6 %all-to-all-start.1 = ((f32[16,32,1040]{2,1,0:T(8,128)}), f32[16,32,1040]{2,1,0:T(8,128)S(1)}, u32[]{:S(2)}, u32[]{:S(2)}) async-start(f32[16,32,1040]{2,1,0:T(8,128)} %bitcast.39), calls=%async_computation.1 | async-start | bytes 4718592 | tf_op jit(solution)/shard_map/all_to_all | solution.py:207
  57.7 1.1 broadcast_select_fusion.2
  58.8 1.3 %collective-permute-start.3 = (bf16[2,1024,128]{2,1,0:T(8,128)(2,1)S(1)}, bf16[2,1024,128]{2,1,0:T(8,128)(2,1)S(1)}, u32[]{:S(2)}, u32[]{:S(2)}) collective-permute-start(bf16[2,1024,128]{2,1,0:T(8,128)(2,1)S(1)} %broadcast_select_fusion.2), channel_id=1, source_target_pairs={{0,8},{16,24},{32,40},{48,56},{64,72},{80,88},{96,104},{112,120},{... | collective-permute-start | bytes 1572872 | tf_op jit(solution)/shard_map/ppermute | solution.py:174
  60.1 1.9 %fusion.9 = (f32[32,8]{0,1:T(8,128)S(1)}, f32[32,8,512]{2,0,1:T(8,128)}) fusion(bf16[512,1280]{1,0:T(8,128)(2,1)} %bitcast.47, pred[32,512]{1,0:T(8,128)(4,1)S(1)} %fusion.8, bf16[32,1024]{1,0:T(8,128)(2,1)S(1)} %copy-done.4), kind=kOutput, calls=%fused_computation.26 | convolution fusion | flops 33947392 | bytes 738304 | tf_op jit(solution)/shard_map/rhd,kd->rhk/dot_general | solution.py:223
  62.1 1.9 %fusion.2 = (f32[32,8]{0,1:T(8,128)}, bf16[32,8,512]{2,0,1:T(8,128)(2,1)S(1)}) fusion(f32[32,8,512]{2,0,1:T(8,128)} %get-tuple-element.15, f32[32,8]{0,1:T(8,128)S(1)} %get-tuple-element.14, pred[32,512]{1,0:T(8,128)(4,1)S(1)} %fusion.8), kind=kLoop, calls=%fused_computation.9 | loop fusion | flops 524032 | bytes 804864 | tf_op jit(solution)/shard_map/reduce_sum | solution.py:227
  64.0 1.2 fusion.4
  65.2 1.4 %copy.17 = f32[32,8]{1,0:T(8,128)} copy(f32[32,8]{0,1:T(8,128)} %get-tuple-element.10) | data formatting | bytes 2048 | tf_op jit(solution)/shard_map/reduce_sum | solution.py:227
  66.5 1.5 %concatenate.7.own_ref = f32[32,1040]{1,0:T(8,128)} concatenate(f32[32,1024]{1,0:T(8,128)S(1)} %bitcast.49, f32[32,8]{1,0:T(8,128)S(1)} %copy.16, f32[32,8]{1,0:T(8,128)} %copy.17), dimensions={1} | concatenate | bytes 266240 | tf_op jit(solution)/shard_map/concatenate | solution.py:231
  68.1 0.8 slice_bitcast_fusion
  68.9 23.4 %shard_map.95.into_ref = f32[1024,1024]{1,0:T(8,128)} custom-call(s32[1]{0:T(128)} %bitcast.flag_ref, bf16[1024,1024]{1,0:T(8,128)(2,1)} %q_ref.3, bf16[1024,128]{1,0:T(8,128)(2,1)} %get-tuple-element.13.ka_ref, bf16[1024,128]{1,0:T(8,128)(2,1)} %get-tuple-element.12.va_ref, bf16[1024,128]{1,0:T(8,128)(2,1)} %ko_ref.3, bf16[1024,128]{1,0:T(8,128)(2,1)} %vo_ref.3), custom_call_target="tpu_custom_call" | custom-call | tf_op jit(solution)/shard_map/pallas_call | solution.py:85
  92.3 1.4 %copy-done = f32[16,32,1040]{2,1,0:T(8,128)} copy-done((f32[16,32,1040]{2,1,0:T(8,128)}, f32[16,32,1040]{2,1,0:T(8,128)S(1)}, u32[]{:S(2)}) %copy-start) | copy-done | bytes 2129944
  93.8 12.3 %shard_map.98 = f32[8,32,1024]{2,1,0:T(8,128)} custom-call(f32[16,32,1040]{2,1,0:T(8,128)} %copy-done, f32[32,1040]{1,0:T(8,128)} %concatenate.7.own_ref, bf16[1024,8192]{1,0:T(8,128)(2,1)} %w_ref.1), custom_call_target="tpu_custom_call" | custom-call | tf_op jit(solution)/shard_map/pallas_call | solution.py:119
  106.1 8.3 %all-to-all-start.2 = ((f32[8,32,1024]{2,1,0:T(8,128)}), f32[8,32,1024]{2,1,0:T(8,128)S(1)}, u32[]{:S(2)}, u32[]{:S(2)}) async-start(f32[8,32,1024]{2,1,0:T(8,128)} %shard_map.98), calls=%async_computation.2 | async-start | bytes 2097152 | tf_op jit(solution)/shard_map/all_to_all | solution.py:234
  114.4 14.9 %shard_map.97 = f32[1024,1024]{1,0:T(8,128)} custom-call(s32[1]{0:T(128)} %bitcast.flag_ref, bf16[1024,1024]{1,0:T(8,128)(2,1)} %q_ref.3, bf16[1024,128]{1,0:T(8,128)(2,1)} %get-tuple-element.13.ka_ref, bf16[1024,128]{1,0:T(8,128)(2,1)} %get-tuple-element.12.va_ref, bf16[1024,128]{1,0:T(8,128)(2,1)} %ko_ref.3, ...), custom_call_target="tpu_custom_call", output_to_operand_aliasing={{}: (6, {})} | custom-call | tf_op jit(solution)/shard_map/pallas_call | solution.py:85
  129.3 0.7 reduce_sum.19
  (25 shorter events, 1.1 us)
Async XLA Ops:
  1.7 11.4 %copy-start.1 = (bf16[1024,128]{1,0:T(8,128)(2,1)S(1)}, bf16[1024,128]{1,0:T(8,128)(2,1)}, u32[]{:S(2)}) copy-start(bf16[1024,128]{1,0:T(8,128)(2,1)} %vo_ref.3) | copy-start | bytes 786436
  1.7 11.4 %copy-start.2 = (bf16[1024,128]{1,0:T(8,128)(2,1)S(1)}, bf16[1024,128]{1,0:T(8,128)(2,1)}, u32[]{:S(2)}) copy-start(bf16[1024,128]{1,0:T(8,128)(2,1)} %ko_ref.3) | copy-start | bytes 786436
  1.8 11.4 %collective-permute-start = (bf16[2,1024,128]{2,1,0:T(8,128)(2,1)S(1)}, bf16[2,1024,128]{2,1,0:T(8,128)(2,1)S(1)}, u32[]{:S(2)}, u32[]{:S(2)}) collective-permute-start(bf16[2,1024,128]{2,1,0:T(8,128)(2,1)S(1)} %pad_maximum_fusion), channel_id=1, source_target_pairs={{0,64},{1,65},{2,66},{3,67},{4,68},{5,69},{6,70},{7,71}} | collective-permute-start | bytes 1572872 | tf_op jit(solution)/shard_map/ppermute | solution.py:174
  4.7 26.5 %all-to-all-start = ((bf16[16,32,1280]{2,1,0:T(8,128)(2,1)}), bf16[16,32,1280]{2,1,0:T(8,128)(2,1)S(1)}, u32[]{:S(2)}, u32[]{:S(2)}) async-start(bf16[16,32,1280]{2,1,0:T(8,128)(2,1)} %broadcast_in_dim.31), calls=%async_computation | async-start | bytes 2621440 | tf_op jit(solution)/shard_map/all_to_all | solution.py:167
  13.3 0.7 collective-permute-start.1
  14.1 43.6 %collective-permute-start.2 = (bf16[2,1024,128]{2,1,0:T(8,128)(2,1)S(1)}, bf16[2,1024,128]{2,1,0:T(8,128)(2,1)}, u32[]{:S(2)}, u32[]{:S(2)}) collective-permute-start(bf16[2,1024,128]{2,1,0:T(8,128)(2,1)S(1)} %broadcast_select_fusion.1), channel_id=1, source_target_pairs={{0,16},{32,48},{64,80},{96,112},{1,17},{33,49},{65,81},{97,113},{2... | collective-permute-start | bytes 1572872 | tf_op jit(solution)/shard_map/ppermute | solution.py:174
  31.1 15.1 %copy-start.3 = (bf16[16,32,1280]{2,1,0:T(8,128)(2,1)}, bf16[16,32,1280]{2,1,0:T(8,128)(2,1)S(1)}, u32[]{:S(2)}) copy-start(bf16[16,32,1280]{2,1,0:T(8,128)(2,1)S(1)} %all-to-all-done) | copy-start | bytes 3932164
  46.2 13.9 %copy-start.4 = (bf16[32,1024]{1,0:T(8,128)(2,1)S(1)}, bf16[32,1024]{1,0:T(8,128)(2,1)}, u32[]{:S(2)}) copy-start(bf16[32,1024]{1,0:T(8,128)(2,1)} %param.11) | copy-start | bytes 196612
  46.2 46.1 %all-to-all-start.1 = ((f32[16,32,1040]{2,1,0:T(8,128)}), f32[16,32,1040]{2,1,0:T(8,128)S(1)}, u32[]{:S(2)}, u32[]{:S(2)}) async-start(f32[16,32,1040]{2,1,0:T(8,128)} %bitcast.39), calls=%async_computation.1 | async-start | bytes 4718592 | tf_op jit(solution)/shard_map/all_to_all | solution.py:207
  58.8 9.2 %collective-permute-start.3 = (bf16[2,1024,128]{2,1,0:T(8,128)(2,1)S(1)}, bf16[2,1024,128]{2,1,0:T(8,128)(2,1)S(1)}, u32[]{:S(2)}, u32[]{:S(2)}) collective-permute-start(bf16[2,1024,128]{2,1,0:T(8,128)(2,1)S(1)} %broadcast_select_fusion.2), channel_id=1, source_target_pairs={{0,8},{16,24},{32,40},{48,56},{64,72},{80,88},{96,104},{112,120},{... | collective-permute-start | bytes 1572872 | tf_op jit(solution)/shard_map/ppermute | solution.py:174
  92.3 1.4 %copy-start = (f32[16,32,1040]{2,1,0:T(8,128)}, f32[16,32,1040]{2,1,0:T(8,128)S(1)}, u32[]{:S(2)}) copy-start(f32[16,32,1040]{2,1,0:T(8,128)S(1)} %all-to-all-done.1) | copy-start | bytes 6389764
  106.1 23.2 %all-to-all-start.2 = ((f32[8,32,1024]{2,1,0:T(8,128)}), f32[8,32,1024]{2,1,0:T(8,128)S(1)}, u32[]{:S(2)}, u32[]{:S(2)}) async-start(f32[8,32,1024]{2,1,0:T(8,128)} %shard_map.98), calls=%async_computation.2 | async-start | bytes 2097152 | tf_op jit(solution)/shard_map/all_to_all | solution.py:234

commit v2 on v1

--- a/solution.py
+++ b/solution.py
@@ -57,15 +57,17 @@
             tile(c, False)
 
 
-def ctx_attention(flag, q, ka, va, ko, vo, head0, nheads, into=None, tq=256):
+def ctx_attention(flag, q, anchor, ko, vo, head0, nheads, into=None, tq=256):
     rows, width = q.shape
     block = ko.shape[0]
     kv_spec = pl.BlockSpec((block, HEAD_WIDTH), lambda h, i, f: (0, 0))
     in_specs = [
         pl.BlockSpec((tq, HEAD_WIDTH), lambda h, i, f: (i, h + head0)),
-        kv_spec, kv_spec, kv_spec, kv_spec,
+        pl.BlockSpec((None, block, HEAD_WIDTH), lambda h, i, f: (0, 0, 0)),
+        pl.BlockSpec((None, block, HEAD_WIDTH), lambda h, i, f: (1, 0, 0)),
+        kv_spec, kv_spec,
     ]
-    operands = [flag, q, ka, va, ko, vo]
+    operands = [flag, q, anchor, anchor, ko, vo]
     kernel = _ctx_kernel
     aliases = {}
     if into is not None:
@@ -207,7 +209,7 @@
     state = lax.all_to_all(state, "ctx", 0, 0, tiled=True)
 
     flag = (device > 0).astype(jnp.int32).reshape(1)
-    kv = (anchor[0], anchor[1], context_key_rows, context_value_rows)
+    kv = (anchor, context_key_rows, context_value_rows)
     half = (heads * 5) // 8
     ctx_out = ctx_attention(flag, ctx_queries, *kv, 0, half)
     ctx_out, state = lax.optimization_barrier((ctx_out, state))

time: 132 us -> 158 us (1.20)
  the two profiles are of different devices: /device:TPU:24 before, /device:TPU:26 now
where the time goes in v2:
time: 158 us; the launch traced here: 155 us
  Pallas kernels  64.5 us (41%)
  waiting for transfers between devices  44.2 us (28%)
  starting transfers between devices  28.6 us (18%)
  local copies, waits for them, and re-layouts  6.74 us (4%)
  other arithmetic  6.54 us (4%)
  matrix products  3.12 us (2%)
    pallas_call x2, Pallas kernels, ctx_attention(): pl.pallas_call(kernel, grid_spec=grid_spec, out_shape=jax.ShapeDtypeStruc...  38.4 us
    ppermute x4, waiting for transfers between devices, broadcast_from_first(): got = lax.ppermute(x, axis, pairs)  31.1 us
    pallas_call x1, Pallas kernels, part_attention(): pl.pallas_call(_part_kernel, grid=(rows // tq,), in_specs=[pl.BlockSpec((...  13.9 us
    all_to_all x1, waiting for transfers between devices, gather_by_all_to_all(): lax.all_to_all(copies, axis, 0, 0).reshape((n * x.shape[0],) + x.shape[1:])  13.2 us
    pallas_call x1, Pallas kernels, finish_projection(): pl.pallas_call(_finish_kernel, grid=(cols // tn,), in_specs=[pl.BlockSpec...  12.3 us
    all_to_all x1, starting transfers between devices, gather_by_all_to_all(): lax.all_to_all(copies, axis, 0, 0).reshape((n * x.shape[0],) + x.shape[1:])  8.51 us
    all_to_all x1, starting transfers between devices, layer(): shares = lax.all_to_all(projected, 'tp', 0, 0, tiled=True)  8.28 us
    all_to_all x1, starting transfers between devices, layer(): state = lax.all_to_all(state, 'ctx', 0, 0, tiled=True)  6.96 us
  transfers between devices with their start and end apart: 7, of which 2 were waited for; matrix products, arithmetic and copies ran while one was open for 8% of the time, Pallas kernels for 34%

profile of v2, /device:TPU:26, one launch (start us, length us, event | category | flops | bytes accessed | tf_op | source)
XLA Modules:
  0.0 155.2 jit_solution(3353383486624630474)
XLA Ops:
  0.6 1.1 pad_maximum_fusion
  2.6 0.9 pad_maximum_fusion.1
  3.5 1.2 broadcast_in_dim.31
  4.7 8.5 %all-to-all-start = ((bf16[16,32,1280]{2,1,0:T(8,128)(2,1)}), bf16[16,32,1280]{2,1,0:T(8,128)(2,1)S(1)}, u32[]{:S(2)}, u32[]{:S(2)}) async-start(bf16[16,32,1280]{2,1,0:T(8,128)(2,1)} %broadcast_in_dim.31), calls=%async_computation | async-start | bytes 2621440 | tf_op jit(solution)/shard_map/all_to_all | solution.py:169
  13.2 0.9 broadcast_select_fusion
  14.1 1.4 collective-permute-start.1
  16.1 13.2 %all-to-all-done = bf16[16,32,1280]{2,1,0:T(8,128)(2,1)S(1)} async-done(((bf16[16,32,1280]{2,1,0:T(8,128)(2,1)}), bf16[16,32,1280]{2,1,0:T(8,128)(2,1)S(1)}, u32[]{:S(2)}, u32[]{:S(2)}) %all-to-all-start) | async-done | bytes 1310752 | tf_op jit(solution)/shard_map/all_to_all | solution.py:169
  29.3 1.2 slice.12.q_ref
  30.5 13.9 %shard_map.96 = f32[512,1040]{1,0:T(8,128)} custom-call(bf16[512,1024]{1,0:T(8,128)(2,1)} %slice.12.q_ref, bf16[1024,128]{1,0:T(8,128)(2,1)} %ko_ref.3, bf16[1024,128]{1,0:T(8,128)(2,1)} %vo_ref.3), custom_call_target="tpu_custom_call" | custom-call | tf_op jit(solution)/shard_map/pallas_call | solution.py:157
  44.4 7.0 %all-to-all-start.1 = ((f32[16,32,1040]{2,1,0:T(8,128)}), f32[16,32,1040]{2,1,0:T(8,128)S(1)}, u32[]{:S(2)}, u32[]{:S(2)}) async-start(f32[16,32,1040]{2,1,0:T(8,128)} %bitcast.35), calls=%async_computation.1 | async-start | bytes 4718592 | tf_op jit(solution)/shard_map/all_to_all | solution.py:209
  51.5 1.3 collective-permute-start.2
  52.9 31.1 %collective-permute-done.2 = bf16[2,1024,128]{2,1,0:T(8,128)(2,1)S(1)} collective-permute-done((bf16[2,1024,128]{2,1,0:T(8,128)(2,1)S(1)}, bf16[2,1024,128]{2,1,0:T(8,128)(2,1)S(1)}, u32[]{:S(2)}, u32[]{:S(2)}) %collective-permute-start.2) | collective-permute-done | bytes 524320 | tf_op jit(solution)/shard_map/ppermute | solution.py:176
  84.0 1.3 collective-permute-start.3
  85.4 1.9 %fusion.9 = (f32[32,8]{0,1:T(8,128)S(1)}, f32[32,8,512]{2,0,1:T(8,128)}) fusion(bf16[512,1280]{1,0:T(8,128)(2,1)} %bitcast.43, pred[32,512]{1,0:T(8,128)(4,1)S(1)} %fusion.8, bf16[32,1024]{1,0:T(8,128)(2,1)S(1)} %copy-done.6), kind=kOutput, calls=%fused_computation.24 | convolution fusion | flops 33947392 | bytes 738304 | tf_op jit(solution)/shard_map/rhd,kd->rhk/dot_general | solution.py:225
  87.4 1.9 %fusion.2 = (f32[32,8]{0,1:T(8,128)}, bf16[32,8,512]{2,0,1:T(8,128)(2,1)S(1)}) fusion(f32[32,8,512]{2,0,1:T(8,128)} %get-tuple-element.13, f32[32,8]{0,1:T(8,128)S(1)} %get-tuple-element.12, pred[32,512]{1,0:T(8,128)(4,1)S(1)} %fusion.8), kind=kLoop, calls=%fused_computation.9 | loop fusion | flops 524032 | bytes 804864 | tf_op jit(solution)/shard_map/reduce_sum | solution.py:229
  89.3 1.2 fusion.4
  90.5 1.4 copy.17
  91.8 1.5 concatenate.7.own_ref
  93.3 0.9 broadcast_select_fusion.3.ka_ref.va_ref
  94.1 23.5 %shard_map.95.into_ref = f32[1024,1024]{1,0:T(8,128)} custom-call(s32[1]{0:T(128)} %bitcast.flag_ref, bf16[1024,1024]{1,0:T(8,128)(2,1)} %q_ref.3, bf16[2,1024,128]{2,1,0:T(8,128)(2,1)} %broadcast_select_fusion.3.ka_ref.va_ref, bf16[2,1024,128]{2,1,0:T(8,128)(2,1)} %broadcast_select_fusion.3.ka_ref.va_ref, bf16[1024,128]{1,0:T(8,128)(2,1)} %ko_ref.3, ...), custom_call_target="tpu_custom_call" | custom-call | tf_op jit(solution)/shard_map/pallas_call | solution.py:87
  117.6 1.4 copy-done
  119.1 12.3 %shard_map.98 = f32[8,32,1024]{2,1,0:T(8,128)} custom-call(f32[16,32,1040]{2,1,0:T(8,128)} %copy-done, f32[32,1040]{1,0:T(8,128)} %concatenate.7.own_ref, bf16[1024,8192]{1,0:T(8,128)(2,1)} %w_ref.1), custom_call_target="tpu_custom_call" | custom-call | tf_op jit(solution)/shard_map/pallas_call | solution.py:121
  131.4 8.3 %all-to-all-start.2 = ((f32[8,32,1024]{2,1,0:T(8,128)}), f32[8,32,1024]{2,1,0:T(8,128)S(1)}, u32[]{:S(2)}, u32[]{:S(2)}) async-start(f32[8,32,1024]{2,1,0:T(8,128)} %shard_map.98), calls=%async_computation.2 | async-start | bytes 2097152 | tf_op jit(solution)/shard_map/all_to_all | solution.py:236
  139.7 14.9 %shard_map.97 = f32[1024,1024]{1,0:T(8,128)} custom-call(s32[1]{0:T(128)} %bitcast.flag_ref, bf16[1024,1024]{1,0:T(8,128)(2,1)} %q_ref.3, bf16[2,1024,128]{2,1,0:T(8,128)(2,1)} %broadcast_select_fusion.3.ka_ref.va_ref, bf16[2,1024,128]{2,1,0:T(8,128)(2,1)} %broadcast_select_fusion.3.ka_ref.va_ref, ...), custom_call_target="tpu_custom_call", output_to_operand_aliasing={{}: (6, {})} | custom-call | tf_op jit(solution)/shard_map/pallas_call | solution.py:87
  (28 shorter events, 1.9 us)
Async XLA Ops:
  1.7 11.4 %copy-start.1 = (bf16[1024,128]{1,0:T(8,128)(2,1)S(1)}, bf16[1024,128]{1,0:T(8,128)(2,1)}, u32[]{:S(2)}) copy-start(bf16[1024,128]{1,0:T(8,128)(2,1)} %vo_ref.3) | copy-start | bytes 786436
  1.7 11.4 %copy-start.3 = (bf16[1024,128]{1,0:T(8,128)(2,1)S(1)}, bf16[1024,128]{1,0:T(8,128)(2,1)}, u32[]{:S(2)}) copy-start(bf16[1024,128]{1,0:T(8,128)(2,1)} %ko_ref.3) | copy-start | bytes 786436
  1.8 11.4 %collective-permute-start = (bf16[2,1024,128]{2,1,0:T(8,128)(2,1)S(1)}, bf16[2,1024,128]{2,1,0:T(8,128)(2,1)S(1)}, u32[]{:S(2)}, u32[]{:S(2)}) collective-permute-start(bf16[2,1024,128]{2,1,0:T(8,128)(2,1)S(1)} %pad_maximum_fusion), channel_id=1, source_target_pairs={{0,64},{1,65},{2,66},{3,67},{4,68},{5,69},{6,70},{7,71}} | collective-permute-start | bytes 1572872 | tf_op jit(solution)/shard_map/ppermute | solution.py:176
  4.7 24.6 %all-to-all-start = ((bf16[16,32,1280]{2,1,0:T(8,128)(2,1)}), bf16[16,32,1280]{2,1,0:T(8,128)(2,1)S(1)}, u32[]{:S(2)}, u32[]{:S(2)}) async-start(bf16[16,32,1280]{2,1,0:T(8,128)(2,1)} %broadcast_in_dim.31), calls=%async_computation | async-start | bytes 2621440 | tf_op jit(solution)/shard_map/all_to_all | solution.py:169
  14.1 37.3 %collective-permute-start.1 = (bf16[2,1024,128]{2,1,0:T(8,128)(2,1)}, bf16[2,1024,128]{2,1,0:T(8,128)(2,1)}, u32[]{:S(2)}, u32[]{:S(2)}) collective-permute-start(bf16[2,1024,128]{2,1,0:T(8,128)(2,1)} %broadcast_select_fusion), channel_id=1, source_target_pairs={{0,32},{64,96},{1,33},{65,97},{2,34},{66,98},{3,35},{67,99},{4,36}... | collective-permute-start | bytes 1572872 | tf_op jit(solution)/shard_map/ppermute | solution.py:176
  29.3 15.1 %copy-start.5 = (bf16[16,32,1280]{2,1,0:T(8,128)(2,1)}, bf16[16,32,1280]{2,1,0:T(8,128)(2,1)S(1)}, u32[]{:S(2)}) copy-start(bf16[16,32,1280]{2,1,0:T(8,128)(2,1)S(1)} %all-to-all-done) | copy-start | bytes 3932164
  44.4 7.0 %copy-start.2 = (bf16[1024,128]{1,0:T(8,128)(2,1)S(1)}, bf16[1024,128]{1,0:T(8,128)(2,1)}, u32[]{:S(2)}) copy-start(bf16[1024,128]{1,0:T(8,128)(2,1)} %vo_ref.3) | copy-start | bytes 786436
  44.4 7.0 %copy-start.4 = (bf16[1024,128]{1,0:T(8,128)(2,1)S(1)}, bf16[1024,128]{1,0:T(8,128)(2,1)}, u32[]{:S(2)}) copy-start(bf16[1024,128]{1,0:T(8,128)(2,1)} %ko_ref.3) | copy-start | bytes 786436
  44.4 73.3 %all-to-all-start.1 = ((f32[16,32,1040]{2,1,0:T(8,128)}), f32[16,32,1040]{2,1,0:T(8,128)S(1)}, u32[]{:S(2)}, u32[]{:S(2)}) async-start(f32[16,32,1040]{2,1,0:T(8,128)} %bitcast.35), calls=%async_computation.1 | async-start | bytes 4718592 | tf_op jit(solution)/shard_map/all_to_all | solution.py:209
  51.3 34.0 %copy-start.6 = (bf16[32,1024]{1,0:T(8,128)(2,1)S(1)}, bf16[32,1024]{1,0:T(8,128)(2,1)}, u32[]{:S(2)}) copy-start(bf16[32,1024]{1,0:T(8,128)(2,1)} %param.11) | copy-start | bytes 196612
  51.5 32.5 %collective-permute-start.2 = (bf16[2,1024,128]{2,1,0:T(8,128)(2,1)S(1)}, bf16[2,1024,128]{2,1,0:T(8,128)(2,1)S(1)}, u32[]{:S(2)}, u32[]{:S(2)}) collective-permute-start(bf16[2,1024,128]{2,1,0:T(8,128)(2,1)S(1)} %broadcast_select_fusion.1), channel_id=1, source_target_pairs={{0,16},{32,48},{64,80},{96,112},{1,17},{33,49},{65,81},{97,113},{2... | collective-permute-start | bytes 1572872 | tf_op jit(solution)/shard_map/ppermute | solution.py:176
  84.0 9.3 %collective-permute-start.3 = (bf16[2,1024,128]{2,1,0:T(8,128)(2,1)S(1)}, bf16[2,1024,128]{2,1,0:T(8,128)(2,1)S(1)}, u32[]{:S(2)}, u32[]{:S(2)}) collective-permute-start(bf16[2,1024,128]{2,1,0:T(8,128)(2,1)S(1)} %broadcast_select_fusion.2), channel_id=1, source_target_pairs={{0,8},{16,24},{32,40},{48,56},{64,72},{80,88},{96,104},{112,120},{... | collective-permute-start | bytes 1572872 | tf_op jit(solution)/shard_map/ppermute | solution.py:176
  117.6 1.4 copy-start
  131.4 23.1 %all-to-all-start.2 = ((f32[8,32,1024]{2,1,0:T(8,128)}), f32[8,32,1024]{2,1,0:T(8,128)S(1)}, u32[]{:S(2)}, u32[]{:S(2)}) async-start(f32[8,32,1024]{2,1,0:T(8,128)} %shard_map.98), calls=%async_computation.2 | async-start | bytes 2097152 | tf_op jit(solution)/shard_map/all_to_all | solution.py:236
